TPU v7x, 32 devices: a whole 2x2x4 slice. The times are simulated.
32 devices in a mesh: tok: 4 (over y, x), ka: 4 (over z), out: 2 (over core).
Axes of the slice: x: 2, y: 2, z: 4, core: 2. Of those that a mesh axis runs over, the one named last changes fastest.
Arguments:
- features: bfloat16 [1024, 12288], P('tok', ('ka', 'out')), may hold values from -12 to 12, as said below
- lengths: int32 [4], P('tok'), may hold values from 1 to 256, 768 in all
- w_qkv: bfloat16 [12288, 24576], P(('ka', 'tok'), 'out'), may hold values from -0.0546875 to 0.0546875
- b_qkv: bfloat16 [24576], P(('out', 'ka')), may hold values from -2 to 2
- w_out: bfloat16 [8192, 12288], P(('out', 'tok'), 'ka'), may hold values from -0.0625 to 0.0625
- b_out: bfloat16 [12288], P(('ka', 'out')), may hold values from -3 to 3
Outputs:
- result: float32 [1024, 12288], P('tok', ('ka', 'out'))
Inputs may be any that keep to these rules, and one draw needn't show every extreme that they name: features: activations of order one; rows may differ in scale. `lengths`: live tokens of each prompt; some prompt is full.
All inputs are finite; a program needn't handle non-finite values. No bound on the sum of `lengths` on one device may be relied on, other than what follows from the above.
Results may differ from a plain program's by a relative error of at most 0.008.
Values may be sent and summed in bfloat16 or wider, within the bound.
No kernel may reach another device: no remote copies, remote signals or barrier semaphores. Data moves between devices by JAX's collectives and lax.ppermute only.
A program may use at most 192 MiB of HBM per device.

v0:
```python
import jax
import jax.numpy as jnp
from jax import lax
from jax.sharding import PartitionSpec as P

HD = 128
SEQ = 256


def softmax_rows(scores, allowed):
    scores = jnp.where(allowed, scores, -1e30)
    row_max = jnp.max(scores, axis=-1, keepdims=True)
    weights = jnp.exp(scores - row_max)
    row_sum = jnp.sum(weights, axis=-1, keepdims=True)
    return (weights / row_sum).astype(jnp.bfloat16)


def attention(qkv_held, lengths):
    prompts = qkv_held.shape[0] // SEQ
    heads_dev = qkv_held.shape[1] // (3 * HD)
    table = qkv_held.reshape(prompts, SEQ, heads_dev, 3, HD)
    positions = jnp.arange(SEQ)
    causal = positions[None, :] <= positions[:, None]
    live = positions[None, :] < lengths[:, None]
    allowed = causal[None, None] & live[:, None, None, :]
    scores = jnp.einsum(
        "pshd,pthd->phst", table[:, :, :, 0], table[:, :, :, 1], preferred_element_type=jnp.float32
    ) * (1.0 / HD**0.5)
    prob_rows = softmax_rows(scores, allowed)
    context = jnp.einsum(
        "phst,pthd->pshd", prob_rows, table[:, :, :, 2], preferred_element_type=jnp.float32
    )
    return context.astype(jnp.bfloat16).reshape(prompts * SEQ, heads_dev * HD)


def shards(features, lengths, w_qkv, b_qkv, w_out, b_out, n_tok, n_ka, n_out):
    t = lax.axis_index("tok")
    k = lax.axis_index("ka")
    rows_dev = features.shape[0]
    slab = lax.all_gather(features, "out", axis=1, tiled=True)
    chunk = slab.shape[1] // n_tok
    if n_tok & n_tok - 1 == 0:
        pieces = [None] * n_tok
        pieces[0] = lax.dynamic_slice_in_dim(slab, t * chunk, chunk, axis=1)
        for s in range(1, n_tok):
            owed = lax.dynamic_slice_in_dim(slab, jnp.bitwise_xor(t, s) * chunk, chunk, axis=1)
            pieces[s] = lax.ppermute(owed, "tok", [(i, i ^ s) for i in range(n_tok)])
        stacked = jnp.stack(pieces)
        panel = jnp.take(stacked, jnp.bitwise_xor(t, jnp.arange(n_tok)), axis=0)
        panel = panel.reshape(n_tok * rows_dev, chunk)
    else:
        panel = lax.all_to_all(slab, "tok", split_axis=1, concat_axis=0, tiled=True)
    tokens = panel.shape[0]
    n_blocks = tokens // rows_dev
    by_xor = n_blocks == n_ka and n_ka & n_ka - 1 == 0
    if by_xor:
        order = jnp.bitwise_xor(k, jnp.arange(n_blocks))
        panel = jnp.take(panel.reshape(n_blocks, rows_dev, -1), order, axis=0)
        panel = panel.reshape(tokens, -1)
        prompt_of = jnp.bitwise_xor(k, lax.broadcasted_iota(jnp.int32, (tokens, 1), 0) // rows_dev)
    else:
        prompt_of = lax.broadcasted_iota(jnp.int32, (tokens, 1), 0) // rows_dev
    cols = w_qkv.shape[1]
    width = cols // n_tok
    if n_tok == n_ka:
        transpose = [(a * n_ka + b, b * n_ka + a) for a in range(n_tok) for b in range(n_ka)]
        own_lengths = lax.ppermute(lengths, ("tok", "ka"), transpose)
    else:
        all_lengths = lax.all_gather(lengths, "tok", axis=0, tiled=True)
        per = all_lengths.shape[0] // n_ka
        own_lengths = lax.dynamic_slice_in_dim(all_lengths, k * per, per)
    heads_block = width // (3 * HD)
    n_streams = 2 if heads_block % 2 == 0 else 1
    piece = width // n_streams
    own_rows = prompt_of == t
    bias = b_qkv.astype(jnp.float32)
    w_rows = w_out.shape[0] // n_streams
    col_block = lax.broadcasted_iota(jnp.int32, (1, n_tok * piece), 1) // piece
    here = own_rows & (col_block == k)
    terms = None
    for h in range(n_streams):
        w_h = jnp.concatenate(
            [w_qkv[:, c * width + h * piece : c * width + (h + 1) * piece] for c in range(n_tok)],
            axis=1,
        )
        value = jnp.dot(panel, w_h, preferred_element_type=jnp.float32)
        bias_row = jnp.tile(bias[h * piece : (h + 1) * piece], n_tok)[None, :]
        part = (value + jnp.where(here, bias_row, 0.0)).astype(jnp.bfloat16)
        slab_sum = lax.psum_scatter(part, "tok", scatter_dimension=1, tiled=True)
        if by_xor:
            blocks = slab_sum.reshape(n_blocks, rows_dev, piece)
            total = blocks[0].astype(jnp.float32)
            for s in range(1, n_ka):
                pairs = [(i, i ^ s) for i in range(n_ka)]
                total = total + lax.ppermute(blocks[s], "ka", pairs).astype(jnp.float32)
            qkv_held = total.astype(jnp.bfloat16)
        else:
            qkv_held = lax.psum_scatter(slab_sum, "ka", scatter_dimension=0, tiled=True)
        context = attention(qkv_held, own_lengths)
        head_group = lax.all_gather(context, "ka", axis=0, tiled=True)
        term = jnp.einsum(
            "tsd,doc->tosc",
            head_group.reshape(n_tok, tokens // n_tok, -1),
            w_out[h * w_rows : (h + 1) * w_rows].reshape(w_rows, n_out, -1),
            preferred_element_type=jnp.float32,
        )
        terms = term if terms is None else terms + term
    terms = terms.reshape(n_tok * n_out, tokens // n_tok, -1)
    summed = lax.psum_scatter(terms, ("tok", "out"), scatter_dimension=0, tiled=True)
    return summed[0] + b_out.astype(jnp.float32)


def solution(mesh):
    n_tok, n_ka, n_out = (mesh.shape["tok"], mesh.shape["ka"], mesh.shape["out"])
    placed = (
        P("tok", ("ka", "out")),
        P("tok"),
        P(("ka", "tok"), "out"),
        P(("out", "ka")),
        P(("out", "tok"), "ka"),
        P(("ka", "out")),
    )

    def body(*args):
        return shards(*args, n_tok=n_tok, n_ka=n_ka, n_out=n_out)

    return jax.shard_map(
        body, mesh=mesh, in_specs=placed, out_specs=P("tok", ("ka", "out")), check_vma=False
    )
```

profile of v0, /device:TPU:0, one launch (start us, length us, event | category | flops | bytes accessed | tf_op | source)
XLA Modules:
  0.0 550.3 jit_solution(7277942607117833040)
XLA Ops:
  6.5 0.7 all-gather.4.cloned.1.call-update
  7.3 0.8 fusion.48
  8.2 13.5 %fusion.44 = (bf16[768,1536]{1,0:T(8,128)(2,1)}, bf16[768,1536]{1,0:T(8,128)(2,1)}, bf16[768,1536]{1,0:T(8,128)(2,1)}, bf16[768,1536]{1,0:T(8,128)(2,1)}, bf16[7...) fusion(bf16[768,12288]{1,0:T(8,128)(2,1)} %param.10), kind=kLoop, calls=%fused_computation.87 | loop fusion | bytes 37748736 | tf_op jit(solution)/shard_map/slice | solution.py:83
  21.7 1.5 dynamic-slice_bitcast_fusion
  23.2 3.0 collective-permute-start
  26.2 1.5 collective-permute-start.1
  27.8 8.4 %collective-permute-done = bf16[256,768]{1,0:T(8,128)(2,1)S(1)} collective-permute-done((bf16[256,768]{1,0:T(8,128)(2,1)S(1)}, bf16[256,768]{1,0:T(8,128)(2,1)S(1)}, u32[]{:S(2)}, u32[]{:S(2)}) %collective-permute-start) | collective-permute-done | bytes 393248 | tf_op jit(solution)/shard_map/ppermute | solution.py:47
  36.2 9.0 %collective-permute-done.1 = bf16[256,768]{1,0:T(8,128)(2,1)S(1)} collective-permute-done((bf16[256,768]{1,0:T(8,128)(2,1)S(1)}, bf16[256,768]{1,0:T(8,128)(2,1)S(1)}, u32[]{:S(2)}, u32[]{:S(2)}) %collective-permute-start.1) | collective-permute-done | bytes 393248 | tf_op jit(solution)/shard_map/ppermute | solution.py:47
  45.4 0.6 gather_fusion
  46.1 1.4 broadcast_select_fusion.1
  47.4 2.1 gather_fusion.1
  49.7 17.9 %fusion.3 = bf16[1024,6144]{1,0:T(8,128)(2,1)} fusion(bf16[1024,768]{1,0:T(8,128)(2,1)S(1)} %bitcast.100, f32[6144]{0:T(1024)S(1)} %broadcast_in_dim.64, pred[6144]{0:T(1024)(128)(4,1)S(1)} %fusion.27, pred[1024]{0:T(1024)(128)(4,1)S(1)} %fusion.32, bf16[768,1536]{1,0:T(8,128)(2,1)} %get-tuple-element.8, bf16[768,1536]{1,0:T(8,128)(2,1)} %get-tuple-element.9, ...), kind=kOutput, calls=%fused_computation.7 | convolution fusion | flops 9726590976 | bytes 23624704 | tf_op jit(solution)/shard_map/dot_general | solution.py:86
  68.0 1.4 copy-done
  69.3 17.1 %fusion.5 = bf16[1024,6144]{1,0:T(8,128)(2,1)} fusion(bf16[1024,768]{1,0:T(8,128)(2,1)} %bitcast.101, f32[6144]{0:T(1024)S(1)} %broadcast_in_dim.69, pred[6144]{0:T(1024)(128)(4,1)S(1)} %fusion.27, pred[1024]{0:T(1024)(128)(4,1)S(1)} %fusion.32, bf16[768,1536]{1,0:T(8,128)(2,1)} %get-tuple-element.12, bf16[768,1536]{1,0:T(8,128)(2,1)} %get-tuple-element.13, ...), kind=kOutput, calls=%fused_computation.9 | convolution fusion | flops 9726590976 | bytes 23624704 | tf_op jit(solution)/shard_map/dot_general | solution.py:86
  86.5 1.9 collective-permute-start.6
  88.4 100.6 %reduce-scatter.4.cloned.1.call-done = bf16[1024,1536]{1,0:T(8,128)(2,1)} async-done(((bf16[1024,6144]{1,0:T(8,128)(2,1)}), bf16[1024,1536]{1,0:T(8,128)(2,1)}) %reduce-scatter.4.cloned.1.call-update) | async-done | bytes 3145744 | tf_op jit(solution)/shard_map/reduce_scatter | solution.py:89
  188.9 1.8 fusion.47
  190.7 1.5 collective-permute-start.3
  192.2 2.4 collective-permute-start.4
  194.7 0.5 collective-permute-start.5
  195.2 0.7 iota_compare_fusion.1
  196.0 116.8 %reduce-scatter.6.cloned.1.call-done = bf16[1024,1536]{1,0:T(8,128)(2,1)} async-done(((bf16[1024,6144]{1,0:T(8,128)(2,1)}), bf16[1024,1536]{1,0:T(8,128)(2,1)}) %reduce-scatter.6.cloned.1.call-update) | async-done | bytes 3145744 | tf_op jit(solution)/shard_map/reduce_scatter | solution.py:89
  312.8 3.0 fusion.46
  315.8 1.5 collective-permute-start.7
  317.2 2.4 collective-permute-start.8
  319.7 0.5 collective-permute-start.9
  320.2 2.2 add_convert_fusion.1
  322.4 0.3 copy.17
  322.7 0.6 fusion.49
  323.2 0.4 fusion.25
  323.6 1.1 convolution_convert_fusion.1
  324.8 38.2 %collective-permute-done.7 = bf16[256,1536]{1,0:T(8,128)(2,1)} collective-permute-done((bf16[256,1536]{1,0:T(8,128)(2,1)}, bf16[256,1536]{1,0:T(8,128)(2,1)}, u32[]{:S(2)}, u32[]{:S(2)}) %collective-permute-start.7) | collective-permute-done | bytes 786464 | tf_op jit(solution)/shard_map/ppermute | solution.py:95
  362.9 18.0 %collective-permute-done.8 = bf16[256,1536]{1,0:T(8,128)(2,1)} collective-permute-done((bf16[256,1536]{1,0:T(8,128)(2,1)}, bf16[256,1536]{1,0:T(8,128)(2,1)}, u32[]{:S(2)}, u32[]{:S(2)}) %collective-permute-start.8) | collective-permute-done | bytes 786464 | tf_op jit(solution)/shard_map/ppermute | solution.py:95
  380.9 2.3 add_convert_fusion
  383.4 0.6 fusion.50
  384.0 0.4 fusion.24
  384.3 1.1 convolution_convert_fusion
  385.8 4.9 fusion.45
  390.7 2.8 copy.44
  393.5 3.2 copy.48
  396.7 2.3 copy.22
  399.0 10.2 %fusion.51 = f32[4,256,2,1536]{3,1,2,0:T(8,128)} fusion(bf16[4,256,512,1]{2,1,3,0:T(8,128)(2,1)} %bitcast.102, bf16[512,2,1536,1]{0,2,1,3:T(8,128)(2,1)} %bitcast.93), kind=kOutput, calls=%fused_computation.94 | convolution fusion | flops 3221225472 | bytes 16777216 | tf_op jit(solution)/shard_map/tsd,doc->tosc/dot_general | solution.py:101
  409.2 28.8 %all-gather.8.cloned.1.call-done = bf16[1024,512]{0,1:T(8,128)(2,1)} async-done(((bf16[256,512]{0,1:T(8,128)(2,1)}), bf16[1024,512]{0,1:T(8,128)(2,1)}) %all-gather.8.cloned.1.call-update) | async-done | bytes 1048592 | tf_op jit(solution)/shard_map/all_gather | solution.py:100
  438.0 2.3 copy.30
  440.3 9.5 %convolution_add_fusion = f32[4,256,2,1536]{3,1,2,0:T(8,128)} fusion(f32[4,256,2,1536]{3,1,2,0:T(8,128)} %fusion.51, bf16[4,256,512,1]{2,1,3,0:T(8,128)(2,1)} %bitcast.92, bf16[512,2,1536,1]{0,2,1,3:T(8,128)(2,1)S(1)} %bitcast.91), kind=kOutput, calls=%fused_computation.24 | convolution fusion | flops 3224371200 | bytes 29360128 | tf_op jit(solution)/shard_map/tsd,doc->tosc/dot_general | solution.py:101
  449.8 0.7 copy-done.2
  450.5 90.2 %reduce-scatter.8.cloned.1.call-done = f32[1,256,1536]{2,1,0:T(8,128)} async-done(((f32[8,256,1536]{2,1,0:T(8,128)}), f32[1,256,1536]{2,1,0:T(8,128)}) %reduce-scatter.8.cloned.1.call-update) | async-done | bytes 1572880 | tf_op jit(solution)/shard_map/reduce_scatter | solution.py:109
  540.7 2.7 bitcast_add_fusion
  (40 shorter events, 1.7 us)
Async XLA Ops:
  6.5 15.2 %all-gather.4.cloned.1.call-start = ((), (), s32[]{:S(2)}) async-start(), calls=%async_computation.3 | async-start | bytes 2359296 | tf_op jit(solution)/shard_map/all_gather | solution.py:40
  7.3 181.7 %reduce-scatter.4.cloned.1.call-start = ((), (), s32[]{:S(2)}) async-start(), calls=%async_computation.4 | async-start | bytes 15728640 | tf_op jit(solution)/shard_map/reduce_scatter | solution.py:89
  23.2 13.0 %collective-permute-start = (bf16[256,768]{1,0:T(8,128)(2,1)S(1)}, bf16[256,768]{1,0:T(8,128)(2,1)S(1)}, u32[]{:S(2)}, u32[]{:S(2)}) collective-permute-start(bf16[256,768]{1,0:T(8,128)(2,1)S(1)} %get-tuple-element.25), channel_id=1, source_target_pairs={{0,8},{8,0},{16,24},{24,16},{1,9},{9,1},{17,25},{25,17},{2,10},{10... | collective-permute-start | bytes 1179656 | tf_op jit(solution)/shard_map/ppermute | solution.py:47
  26.2 19.0 %collective-permute-start.1 = (bf16[256,768]{1,0:T(8,128)(2,1)S(1)}, bf16[256,768]{1,0:T(8,128)(2,1)S(1)}, u32[]{:S(2)}, u32[]{:S(2)}) collective-permute-start(bf16[256,768]{1,0:T(8,128)(2,1)S(1)} %get-tuple-element.24), channel_id=1, source_target_pairs={{0,16},{8,24},{16,0},{24,8},{1,17},{9,25},{17,1},{25,9},{2,18},{10... | collective-permute-start | bytes 1179656 | tf_op jit(solution)/shard_map/ppermute | solution.py:47
  27.8 17.5 %collective-permute-start.2 = (bf16[256,768]{1,0:T(8,128)(2,1)S(1)}, bf16[256,768]{1,0:T(8,128)(2,1)S(1)}, u32[]{:S(2)}, u32[]{:S(2)}) collective-permute-start(bf16[256,768]{1,0:T(8,128)(2,1)S(1)} %get-tuple-element.23), channel_id=1, source_target_pairs={{0,24},{8,16},{16,8},{24,0},{1,25},{9,17},{17,9},{25,1},{2,26},{10... | collective-permute-start | bytes 1179656 | tf_op jit(solution)/shard_map/ppermute | solution.py:47
  49.7 17.9 %copy-start.1 = (bf16[4,256,768]{2,1,0:T(8,128)(2,1)}, bf16[4,256,768]{2,1,0:T(8,128)(2,1)S(1)}, u32[]{:S(2)}) copy-start(bf16[4,256,768]{2,1,0:T(8,128)(2,1)S(1)} %broadcast_select_fusion) | copy-start | bytes 4718596
  67.7 1.7 copy-start
  67.7 245.1 %reduce-scatter.6.cloned.1.call-start = ((), (), s32[]{:S(2)}) async-start(), calls=%async_computation.6 | async-start | bytes 15728640 | tf_op jit(solution)/shard_map/reduce_scatter | solution.py:89
  86.4 310.3 %all-gather.6.cloned.1.call-start = ((), (), s32[]{:S(2)}) async-start(), calls=%async_computation.5 | async-start | bytes 1310720 | tf_op jit(solution)/shard_map/all_gather | solution.py:100
  86.5 108.7 %collective-permute-start.6 = (s32[1]{0:T(128)}, s32[1]{0:T(128)}, u32[]{:S(2)}, u32[]{:S(2)}) collective-permute-start(s32[1]{0:T(128)} %param.9), channel_id=1, source_target_pairs={{0,0},{2,8},{4,16},{6,24},{8,2},{10,10},{12,18},{14,26},{16,4},{18... | collective-permute-start | bytes 20 | tf_op jit(solution)/shard_map/ppermute | solution.py:67
  190.7 129.0 %collective-permute-start.3 = (bf16[256,1536]{1,0:T(8,128)(2,1)S(1)}, bf16[256,1536]{1,0:T(8,128)(2,1)}, u32[]{:S(2)}, u32[]{:S(2)}) collective-permute-start(bf16[256,1536]{1,0:T(8,128)(2,1)S(1)} %get-tuple-element.19), channel_id=1, source_target_pairs={{0,2},{2,0},{4,6},{6,4},{1,3},{3,1},{5,7},{7,5},{8,10},{10,8},{12,... | collective-permute-start | bytes 2359304 | tf_op jit(solution)/shard_map/ppermute | solution.py:95
  192.2 127.9 %collective-permute-start.4 = (bf16[256,1536]{1,0:T(8,128)(2,1)S(1)}, bf16[256,1536]{1,0:T(8,128)(2,1)}, u32[]{:S(2)}, u32[]{:S(2)}) collective-permute-start(bf16[256,1536]{1,0:T(8,128)(2,1)S(1)} %get-tuple-element.21), channel_id=1, source_target_pairs={{0,4},{2,6},{4,0},{6,2},{1,5},{3,7},{5,1},{7,3},{8,12},{10,14},{12... | collective-permute-start | bytes 2359304 | tf_op jit(solution)/shard_map/ppermute | solution.py:95
  194.7 125.5 %collective-permute-start.5 = (bf16[256,1536]{1,0:T(8,128)(2,1)S(1)}, bf16[256,1536]{1,0:T(8,128)(2,1)}, u32[]{:S(2)}, u32[]{:S(2)}) collective-permute-start(bf16[256,1536]{1,0:T(8,128)(2,1)S(1)} %get-tuple-element.20), channel_id=1, source_target_pairs={{0,6},{2,4},{4,2},{6,0},{1,7},{3,5},{5,3},{7,1},{8,14},{10,12},{12... | collective-permute-start | bytes 2359304 | tf_op jit(solution)/shard_map/ppermute | solution.py:95
  315.8 47.2 %collective-permute-start.7 = (bf16[256,1536]{1,0:T(8,128)(2,1)}, bf16[256,1536]{1,0:T(8,128)(2,1)}, u32[]{:S(2)}, u32[]{:S(2)}) collective-permute-start(bf16[256,1536]{1,0:T(8,128)(2,1)} %get-tuple-element.16), channel_id=1, source_target_pairs={{0,2},{2,0},{4,6},{6,4},{1,3},{3,1},{5,7},{7,5},{8,10},{10,8},{12,... | collective-permute-start | bytes 2359304 | tf_op jit(solution)/shard_map/ppermute | solution.py:95
  317.2 63.7 %collective-permute-start.8 = (bf16[256,1536]{1,0:T(8,128)(2,1)}, bf16[256,1536]{1,0:T(8,128)(2,1)}, u32[]{:S(2)}, u32[]{:S(2)}) collective-permute-start(bf16[256,1536]{1,0:T(8,128)(2,1)} %get-tuple-element.18), channel_id=1, source_target_pairs={{0,4},{2,6},{4,0},{6,2},{1,5},{3,7},{5,1},{7,3},{8,12},{10,14},{12... | collective-permute-start | bytes 2359304 | tf_op jit(solution)/shard_map/ppermute | solution.py:95
  319.7 61.2 %collective-permute-start.9 = (bf16[256,1536]{1,0:T(8,128)(2,1)S(1)}, bf16[256,1536]{1,0:T(8,128)(2,1)}, u32[]{:S(2)}, u32[]{:S(2)}) collective-permute-start(bf16[256,1536]{1,0:T(8,128)(2,1)S(1)} %get-tuple-element.17), channel_id=1, source_target_pairs={{0,6},{2,4},{4,2},{6,0},{1,7},{3,5},{5,3},{7,1},{8,14},{10,12},{12... | collective-permute-start | bytes 2359304 | tf_op jit(solution)/shard_map/ppermute | solution.py:95
  324.7 113.3 %all-gather.8.cloned.1.call-start = ((), (), s32[]{:S(2)}) async-start(), calls=%async_computation.7 | async-start | bytes 1310720 | tf_op jit(solution)/shard_map/all_gather | solution.py:100
  385.5 155.2 %reduce-scatter.8.cloned.1.call-start = ((), (), s32[]{:S(2)}) async-start(), calls=%async_computation.8 | async-start | bytes 14155776 | tf_op jit(solution)/shard_map/reduce_scatter | solution.py:109
  449.8 0.7 copy-start.2
Sparse Core Ops, SparseCore 0:
  8.9 12.4 all-gather.3
  67.8 121.0 reduce-scatter.3
  192.0 120.7 reduce-scatter.5
  324.8 70.7 all-gather.5
  397.0 40.9 all-gather.7
  450.0 90.7 reduce-scatter.7
where the time goes:
time: 551 us; the launch traced here: 550 us
  waiting for transfers between devices  411 us (75%)
  matrix products  58.7 us (11%)
  local copies, waits for them, and re-layouts  41.3 us (7%)
  starting transfers between devices  15.9 us (3%)
  between operations  13.7 us (2%)
  other arithmetic  9.85 us (2%)
    reduce_scatter x2, waiting for transfers between devices, shards(): slab_sum = lax.psum_scatter(part, 'tok', scatter_dimension=1, tiled=True)  217 us
    reduce_scatter x1, waiting for transfers between devices, shards(): lax.psum_scatter(terms, ('tok', 'out'), scatter_dimension=0, tiled=True)  90.2 us
    ppermute x6, waiting for transfers between devices, shards(): total = total + lax.ppermute(blocks[s], 'ka', pairs).astype(jnp.float32)  56.1 us
    dot_general x2, matrix products, shards(): value = jnp.dot(panel, w_h, preferred_element_type=jnp.float32)  35 us
    all_gather x2, waiting for transfers between devices, shards(): head_group = lax.all_gather(context, 'ka', axis=0, tiled=True)  28.8 us
    dot_general x2, matrix products, shards(): jnp.einsum('tsd,doc->tosc', head_group.reshape(n_tok, tokens // n_tok, -1...  19.7 us
    ppermute x3, waiting for transfers between devices, shards(): pieces[s] = lax.ppermute(owed, 'tok', [(i, i ^ s) for i in range(n_tok)])  17.4 us
    slice x1, local copies, waits for them, and re-layouts, shards(): w_qkv[:, c * width + h * piece:c * width + (h + 1) * piece]  13.5 us
  transfers between devices with their start and end apart: 16, of which 8 were waited for; matrix products, arithmetic and copies ran while one was open for 13% of the time, Pallas kernels for 0%

commit v1 on v0

--- a/solution.py
+++ b/solution.py
@@ -97,7 +97,24 @@
         else:
             qkv_held = lax.psum_scatter(slab_sum, "ka", scatter_dimension=0, tiled=True)
         context = attention(qkv_held, own_lengths)
-        head_group = lax.all_gather(context, "ka", axis=0, tiled=True)
+        n_parts = lax.axis_size("ka")
+        in_order = []
+        for dd in range(n_parts):
+            in_order.append((dd, (dd + 1) % n_parts))
+        pool = []
+        for dd in range(n_parts):
+            pool.append((dd, (dd - 1) % n_parts))
+        h_now, answer = ([context], [context])
+        for _ in range(n_parts // 2):
+            q_next = lax.ppermute(h_now[-1], "ka", in_order)
+            h_now.append(q_next)
+        for _ in range((n_parts - 1) // 2):
+            reached = lax.ppermute(answer[-1], "ka", pool)
+            answer.append(reached)
+        value_now = jnp.concatenate([*h_now[::-1], *answer[1:]], 0)
+        head_group = jnp.roll(
+            value_now, (lax.axis_index("ka") - n_parts // 2) * context.shape[0], 0
+        )
         term = jnp.einsum(
             "tsd,doc->tosc",
             head_group.reshape(n_tok, tokens // n_tok, -1),

time: 551 us -> 545 us (0.989)
  waiting for transfers between devices: 411 us -> 378 us
  starting transfers between devices: 15.9 us -> 46.4 us
  matrix products: 58.7 us -> 51.3 us
  other arithmetic: 9.85 us -> 15.7 us
    ppermute x0 -> x6, starting transfers between devices: none -> 30.8 us  [the longest x4 24 us: shards(): q_next = lax.ppermute(h_now[-1], 'ka', in_order)]
    all_gather x2 -> x0, waiting for transfers between devices: 28.8 us -> none  [shards(): head_group = lax.all_gather(context, 'ka', axis=0, tiled=True)]
    dot_general x2, matrix products: 19.7 us -> 12.2 us  [shards(): jnp.einsum('tsd,doc->tosc', head_group.reshape(n_tok, tokens // n_tok, -1...]
    concatenate x0 -> x2, other arithmetic: none -> 7.06 us  [shards(): jnp.roll(value_now, (lax.axis_index('ka') - n_parts // 2) * context.shape...]
    ppermute x6, waiting for transfers between devices: 56.1 us -> 49.8 us  [shards(): total = total + lax.ppermute(blocks[s], 'ka', pairs).astype(jnp.float32)]
  transfers between devices with their start and end apart: 16 -> 20, of which waited for: 8 -> 8; matrix products, arithmetic and copies ran while one was open for 13% -> 12% of each run, Pallas kernels for 0% -> 0%
where the time goes in v1:
time: 545 us
  waiting for transfers between devices  378 us (69%)
  matrix products  51.3 us (9%)
  starting transfers between devices  46.4 us (9%)
  local copies, waits for them, and re-layouts  39.9 us (7%)
  other arithmetic  15.7 us (3%)
  between operations  13.4 us (2%)
    reduce_scatter x2, waiting for transfers between devices, shards(): slab_sum = lax.psum_scatter(part, 'tok', scatter_dimension=1, tiled=True)  217 us
    reduce_scatter x1, waiting for transfers between devices, shards(): lax.psum_scatter(terms, ('tok', 'out'), scatter_dimension=0, tiled=True)  90 us
    ppermute x6, waiting for transfers between devices, shards(): total = total + lax.ppermute(blocks[s], 'ka', pairs).astype(jnp.float32)  49.8 us
    dot_general x2, matrix products, shards(): value = jnp.dot(panel, w_h, preferred_element_type=jnp.float32)  35.8 us
    ppermute x4, starting transfers between devices, shards(): q_next = lax.ppermute(h_now[-1], 'ka', in_order)  24 us
    ppermute x3, waiting for transfers between devices, shards(): pieces[s] = lax.ppermute(owed, 'tok', [(i, i ^ s) for i in range(n_tok)])  17.4 us
    slice x1, local copies, waits for them, and re-layouts, shards(): w_qkv[:, c * width + h * piece:c * width + (h + 1) * piece]  13.6 us
    dot_general x2, matrix products, shards(): jnp.einsum('tsd,doc->tosc', head_group.reshape(n_tok, tokens // n_tok, -1...  12.2 us
  transfers between devices with their start and end apart: 20, of which 8 were waited for; matrix products, arithmetic and copies ran while one was open for 12% of the time, Pallas kernels for 0%

profile of v1, /device:TPU:0, one launch (start us, length us, event | category | flops | bytes accessed | tf_op | source)
XLA Modules:
  0.0 545.0 jit_solution(5723927375104443321)
XLA Ops:
  6.5 0.7 all-gather.2.cloned.1.call-update
  7.3 0.8 fusion.62
  8.2 13.6 %fusion.58 = (bf16[768,1536]{1,0:T(8,128)(2,1)}, bf16[768,1536]{1,0:T(8,128)(2,1)}, bf16[768,1536]{1,0:T(8,128)(2,1)}, bf16[768,1536]{1,0:T(8,128)(2,1)}, bf16[7...) fusion(bf16[768,12288]{1,0:T(8,128)(2,1)} %param.12), kind=kLoop, calls=%fused_computation.117 | loop fusion | bytes 37748736 | tf_op jit(solution)/shard_map/slice | solution.py:83
  21.8 1.5 dynamic-slice_bitcast_fusion
  23.2 3.1 collective-permute-start
  26.3 1.5 collective-permute-start.1
  27.9 8.4 %collective-permute-done = bf16[256,768]{1,0:T(8,128)(2,1)S(1)} collective-permute-done((bf16[256,768]{1,0:T(8,128)(2,1)S(1)}, bf16[256,768]{1,0:T(8,128)(2,1)S(1)}, u32[]{:S(2)}, u32[]{:S(2)}) %collective-permute-start) | collective-permute-done | bytes 393248 | tf_op jit(solution)/shard_map/ppermute | solution.py:47
  36.2 9.0 %collective-permute-done.1 = bf16[256,768]{1,0:T(8,128)(2,1)S(1)} collective-permute-done((bf16[256,768]{1,0:T(8,128)(2,1)S(1)}, bf16[256,768]{1,0:T(8,128)(2,1)S(1)}, u32[]{:S(2)}, u32[]{:S(2)}) %collective-permute-start.1) | collective-permute-done | bytes 393248 | tf_op jit(solution)/shard_map/ppermute | solution.py:47
  45.5 0.6 gather_fusion
  46.3 0.6 gather_fusion.1
  47.2 17.9 %fusion.5 = bf16[1024,6144]{1,0:T(8,128)(2,1)} fusion(bf16[1024,768]{1,0:T(8,128)(2,1)S(1)} %bitcast.100, f32[6144]{0:T(1024)S(1)} %broadcast_in_dim.69, pred[6144]{0:T(1024)(128)(4,1)S(1)} %fusion.41, pred[1024]{0:T(1024)(128)(4,1)S(1)} %fusion.46, bf16[768,1536]{1,0:T(8,128)(2,1)} %get-tuple-element.13, bf16[768,1536]{1,0:T(8,128)(2,1)} %get-tuple-element.14, ...), kind=kOutput, calls=%fused_computation.9 | convolution fusion | flops 9726590976 | bytes 23624704 | tf_op jit(solution)/shard_map/dot_general | solution.py:86
  65.4 1.4 copy-done.1
  66.8 17.8 %fusion.3 = bf16[1024,6144]{1,0:T(8,128)(2,1)} fusion(bf16[1024,768]{1,0:T(8,128)(2,1)} %bitcast.101, f32[6144]{0:T(1024)S(1)} %broadcast_in_dim.64, pred[6144]{0:T(1024)(128)(4,1)S(1)} %fusion.41, pred[1024]{0:T(1024)(128)(4,1)S(1)} %fusion.46, bf16[768,1536]{1,0:T(8,128)(2,1)S(1)} %copy-done.1, bf16[768,1536]{1,0:T(8,128)(2,1)} %get-tuple-element.10, ...), kind=kOutput, calls=%fused_computation.7 | convolution fusion | flops 9726590976 | bytes 23624704 | tf_op jit(solution)/shard_map/dot_general | solution.py:86
  84.7 1.9 collective-permute-start.6
  86.6 99.8 %reduce-scatter.6.cloned.1.call-done = bf16[1024,1536]{1,0:T(8,128)(2,1)} async-done(((bf16[1024,6144]{1,0:T(8,128)(2,1)}), bf16[1024,1536]{1,0:T(8,128)(2,1)}) %reduce-scatter.6.cloned.1.call-update) | async-done | bytes 3145744 | tf_op jit(solution)/shard_map/reduce_scatter | solution.py:89
  186.4 1.8 fusion.60
  188.2 1.6 collective-permute-start.10
  189.7 2.4 collective-permute-start.11
  192.6 0.6 iota_compare_fusion.1
  193.4 116.9 %reduce-scatter.4.cloned.1.call-done = bf16[1024,1536]{1,0:T(8,128)(2,1)} async-done(((bf16[1024,6144]{1,0:T(8,128)(2,1)}), bf16[1024,1536]{1,0:T(8,128)(2,1)}) %reduce-scatter.4.cloned.1.call-update) | async-done | bytes 3145744 | tf_op jit(solution)/shard_map/reduce_scatter | solution.py:89
  310.3 2.9 fusion.61
  313.2 1.5 collective-permute-start.3
  314.7 2.4 collective-permute-start.4
  317.1 0.5 collective-permute-start.5
  317.6 2.2 add_convert_fusion
  320.1 0.6 fusion.64
  321.0 1.1 convolution_convert_fusion
  322.1 0.6 collective-permute-start.13
  322.8 3.2 collective-permute-start.15
  326.0 24.0 %collective-permute-done.3 = bf16[256,1536]{1,0:T(8,128)(2,1)} collective-permute-done((bf16[256,1536]{1,0:T(8,128)(2,1)}, bf16[256,1536]{1,0:T(8,128)(2,1)}, u32[]{:S(2)}, u32[]{:S(2)}) %collective-permute-start.3) | collective-permute-done | bytes 786464 | tf_op jit(solution)/shard_map/ppermute | solution.py:95
  350.0 25.8 %collective-permute-done.4 = bf16[256,1536]{1,0:T(8,128)(2,1)} collective-permute-done((bf16[256,1536]{1,0:T(8,128)(2,1)}, bf16[256,1536]{1,0:T(8,128)(2,1)}, u32[]{:S(2)}, u32[]{:S(2)}) %collective-permute-start.4) | collective-permute-done | bytes 786464 | tf_op jit(solution)/shard_map/ppermute | solution.py:95
  375.8 2.2 add_convert_fusion.1
  378.6 0.5 fusion.63
  379.6 23.1 %collective-permute-start.7 = (bf16[256,512]{0,1:T(8,128)(2,1)S(1)}, bf16[256,512]{0,1:T(8,128)(2,1)}, u32[]{:S(2)}, u32[]{:S(2)}) collective-permute-start(bf16[256,512]{0,1:T(8,128)(2,1)S(1)} %bitcast.106), channel_id=1, source_target_pairs={{0,2},{2,4},{4,6},{6,0},{1,3},{3,5},{5,7},{7,1},{8,10},{10,12},{12... | collective-permute-start | bytes 786440 | tf_op jit(solution)/shard_map/ppermute | solution.py:109
  403.0 5.0 fusion.59
  408.0 2.8 copy.44
  410.8 3.2 copy.48
  414.0 3.6 collective-permute-start.9
  417.6 3.6 fusion.29
  421.2 2.3 copy.30
  423.5 3.6 collective-permute-done.8
  427.1 3.4 fusion.36
  430.5 2.3 copy.22
  432.7 5.7 %fusion.65 = f32[4,256,2,1536]{3,1,2,0:T(8,128)S(1)} fusion(bf16[4,256,512,1]{2,1,3,0:T(8,128)(2,1)} %bitcast.102, bf16[512,2,1536,1]{0,2,1,3:T(8,128)(2,1)} %bitcast.93), kind=kOutput, calls=%fused_computation.124 | convolution fusion | flops 3221225472 | bytes 16777216 | tf_op jit(solution)/shard_map/tsd,doc->tosc/dot_general | solution.py:118
  438.5 6.5 %convolution_add_fusion = f32[4,256,2,1536]{3,1,2,0:T(8,128)} fusion(f32[4,256,2,1536]{3,1,2,0:T(8,128)S(1)} %fusion.65, bf16[4,256,512,1]{2,1,3,0:T(8,128)(2,1)S(1)} %bitcast.92, bf16[512,2,1536,1]{0,2,1,3:T(8,128)(2,1)S(1)} %bitcast.91), kind=kOutput, calls=%fused_computation.24 | convolution fusion | flops 3224371200 | bytes 29360128 | tf_op jit(solution)/shard_map/tsd,doc->tosc/dot_general | solution.py:118
  445.0 0.7 copy-done.3
  445.7 90.0 %reduce-scatter.8.cloned.1.call-done = f32[1,256,1536]{2,1,0:T(8,128)} async-done(((f32[8,256,1536]{2,1,0:T(8,128)}), f32[1,256,1536]{2,1,0:T(8,128)}) %reduce-scatter.8.cloned.1.call-update) | async-done | bytes 1572880 | tf_op jit(solution)/shard_map/reduce_scatter | solution.py:126
  535.7 2.7 bitcast_add_fusion
  (50 shorter events, 3.7 us)
Async XLA Ops:
  6.5 15.2 %all-gather.2.cloned.1.call-start = ((), (), s32[]{:S(2)}) async-start(), calls=%async_computation.3 | async-start | bytes 2359296 | tf_op jit(solution)/shard_map/all_gather | solution.py:40
  7.3 179.1 %reduce-scatter.6.cloned.1.call-start = ((), (), s32[]{:S(2)}) async-start(), calls=%async_computation.5 | async-start | bytes 15728640 | tf_op jit(solution)/shard_map/reduce_scatter | solution.py:89
  23.2 13.0 %collective-permute-start = (bf16[256,768]{1,0:T(8,128)(2,1)S(1)}, bf16[256,768]{1,0:T(8,128)(2,1)S(1)}, u32[]{:S(2)}, u32[]{:S(2)}) collective-permute-start(bf16[256,768]{1,0:T(8,128)(2,1)S(1)} %get-tuple-element.26), channel_id=1, source_target_pairs={{0,8},{8,0},{16,24},{24,16},{1,9},{9,1},{17,25},{25,17},{2,10},{10... | collective-permute-start | bytes 1179656 | tf_op jit(solution)/shard_map/ppermute | solution.py:47
  26.3 19.0 %collective-permute-start.1 = (bf16[256,768]{1,0:T(8,128)(2,1)S(1)}, bf16[256,768]{1,0:T(8,128)(2,1)S(1)}, u32[]{:S(2)}, u32[]{:S(2)}) collective-permute-start(bf16[256,768]{1,0:T(8,128)(2,1)S(1)} %get-tuple-element.25), channel_id=1, source_target_pairs={{0,16},{8,24},{16,0},{24,8},{1,17},{9,25},{17,1},{25,9},{2,18},{10... | collective-permute-start | bytes 1179656 | tf_op jit(solution)/shard_map/ppermute | solution.py:47
  27.8 17.4 %collective-permute-start.2 = (bf16[256,768]{1,0:T(8,128)(2,1)S(1)}, bf16[256,768]{1,0:T(8,128)(2,1)S(1)}, u32[]{:S(2)}, u32[]{:S(2)}) collective-permute-start(bf16[256,768]{1,0:T(8,128)(2,1)S(1)} %get-tuple-element.24), channel_id=1, source_target_pairs={{0,24},{8,16},{16,8},{24,0},{1,25},{9,17},{17,9},{25,1},{2,26},{10... | collective-permute-start | bytes 1179656 | tf_op jit(solution)/shard_map/ppermute | solution.py:47
  47.2 17.9 %copy-start.2 = (bf16[4,256,768]{2,1,0:T(8,128)(2,1)}, bf16[4,256,768]{2,1,0:T(8,128)(2,1)S(1)}, u32[]{:S(2)}) copy-start(bf16[4,256,768]{2,1,0:T(8,128)(2,1)S(1)} %broadcast_select_fusion) | copy-start | bytes 4718596
  65.2 1.7 copy-start.1
  65.2 245.1 %reduce-scatter.4.cloned.1.call-start = ((), (), s32[]{:S(2)}) async-start(), calls=%async_computation.4 | async-start | bytes 15728640 | tf_op jit(solution)/shard_map/reduce_scatter | solution.py:89
  84.7 451.0 %reduce-scatter.8.cloned.1.call-start = ((), (), s32[]{:S(2)}) async-start(), calls=%async_computation.6 | async-start | bytes 14155776 | tf_op jit(solution)/shard_map/reduce_scatter | solution.py:126
  84.7 107.9 %collective-permute-start.6 = (s32[1]{0:T(128)}, s32[1]{0:T(128)}, u32[]{:S(2)}, u32[]{:S(2)}) collective-permute-start(s32[1]{0:T(128)} %param.11), channel_id=1, source_target_pairs={{0,0},{2,8},{4,16},{6,24},{8,2},{10,10},{12,18},{14,26},{16,4},{18... | collective-permute-start | bytes 20 | tf_op jit(solution)/shard_map/ppermute | solution.py:67
  188.2 129.0 %collective-permute-start.10 = (bf16[256,1536]{1,0:T(8,128)(2,1)S(1)}, bf16[256,1536]{1,0:T(8,128)(2,1)}, u32[]{:S(2)}, u32[]{:S(2)}) collective-permute-start(bf16[256,1536]{1,0:T(8,128)(2,1)S(1)} %get-tuple-element.17), channel_id=1, source_target_pairs={{0,2},{2,0},{4,6},{6,4},{1,3},{3,1},{5,7},{7,5},{8,10},{10,8},{12,... | collective-permute-start | bytes 2359304 | tf_op jit(solution)/shard_map/ppermute | solution.py:95
  189.7 127.9 %collective-permute-start.11 = (bf16[256,1536]{1,0:T(8,128)(2,1)S(1)}, bf16[256,1536]{1,0:T(8,128)(2,1)}, u32[]{:S(2)}, u32[]{:S(2)}) collective-permute-start(bf16[256,1536]{1,0:T(8,128)(2,1)S(1)} %get-tuple-element.19), channel_id=1, source_target_pairs={{0,4},{2,6},{4,0},{6,2},{1,5},{3,7},{5,1},{7,3},{8,12},{10,14},{12... | collective-permute-start | bytes 2359304 | tf_op jit(solution)/shard_map/ppermute | solution.py:95
  192.1 125.5 %collective-permute-start.12 = (bf16[256,1536]{1,0:T(8,128)(2,1)S(1)}, bf16[256,1536]{1,0:T(8,128)(2,1)}, u32[]{:S(2)}, u32[]{:S(2)}) collective-permute-start(bf16[256,1536]{1,0:T(8,128)(2,1)S(1)} %get-tuple-element.18), channel_id=1, source_target_pairs={{0,6},{2,4},{4,2},{6,0},{1,7},{3,5},{5,3},{7,1},{8,14},{10,12},{12... | collective-permute-start | bytes 2359304 | tf_op jit(solution)/shard_map/ppermute | solution.py:95
  313.2 36.8 %collective-permute-start.3 = (bf16[256,1536]{1,0:T(8,128)(2,1)}, bf16[256,1536]{1,0:T(8,128)(2,1)}, u32[]{:S(2)}, u32[]{:S(2)}) collective-permute-start(bf16[256,1536]{1,0:T(8,128)(2,1)} %get-tuple-element.20), channel_id=1, source_target_pairs={{0,2},{2,0},{4,6},{6,4},{1,3},{3,1},{5,7},{7,5},{8,10},{10,8},{12,... | collective-permute-start | bytes 2359304 | tf_op jit(solution)/shard_map/ppermute | solution.py:95
  314.7 61.1 %collective-permute-start.4 = (bf16[256,1536]{1,0:T(8,128)(2,1)}, bf16[256,1536]{1,0:T(8,128)(2,1)}, u32[]{:S(2)}, u32[]{:S(2)}) collective-permute-start(bf16[256,1536]{1,0:T(8,128)(2,1)} %get-tuple-element.22), channel_id=1, source_target_pairs={{0,4},{2,6},{4,0},{6,2},{1,5},{3,7},{5,1},{7,3},{8,12},{10,14},{12... | collective-permute-start | bytes 2359304 | tf_op jit(solution)/shard_map/ppermute | solution.py:95
  317.1 58.7 %collective-permute-start.5 = (bf16[256,1536]{1,0:T(8,128)(2,1)S(1)}, bf16[256,1536]{1,0:T(8,128)(2,1)}, u32[]{:S(2)}, u32[]{:S(2)}) collective-permute-start(bf16[256,1536]{1,0:T(8,128)(2,1)S(1)} %get-tuple-element.21), channel_id=1, source_target_pairs={{0,6},{2,4},{4,2},{6,0},{1,7},{3,5},{5,3},{7,1},{8,14},{10,12},{12... | collective-permute-start | bytes 2359304 | tf_op jit(solution)/shard_map/ppermute | solution.py:95
  322.1 80.6 %collective-permute-start.13 = (bf16[256,512]{0,1:T(8,128)(2,1)}, bf16[256,512]{0,1:T(8,128)(2,1)}, u32[]{:S(2)}, u32[]{:S(2)}) collective-permute-start(bf16[256,512]{0,1:T(8,128)(2,1)} %bitcast.26), channel_id=1, source_target_pairs={{0,2},{2,4},{4,6},{6,0},{1,3},{3,5},{5,7},{7,1},{8,10},{10,12},{12... | collective-permute-start | bytes 786440 | tf_op jit(solution)/shard_map/ppermute | solution.py:109
  322.8 94.8 %collective-permute-start.15 = (bf16[256,512]{0,1:T(8,128)(2,1)}, bf16[256,512]{0,1:T(8,128)(2,1)}, u32[]{:S(2)}, u32[]{:S(2)}) collective-permute-start(bf16[256,512]{0,1:T(8,128)(2,1)} %bitcast.26), channel_id=1, source_target_pairs={{0,6},{2,0},{4,2},{6,4},{1,7},{3,1},{5,3},{7,5},{8,14},{10,8},{12,... | collective-permute-start | bytes 786440 | tf_op jit(solution)/shard_map/ppermute | solution.py:112
  379.6 37.9 %collective-permute-start.7 = (bf16[256,512]{0,1:T(8,128)(2,1)S(1)}, bf16[256,512]{0,1:T(8,128)(2,1)}, u32[]{:S(2)}, u32[]{:S(2)}) collective-permute-start(bf16[256,512]{0,1:T(8,128)(2,1)S(1)} %bitcast.106), channel_id=1, source_target_pairs={{0,2},{2,4},{4,6},{6,0},{1,3},{3,5},{5,7},{7,1},{8,10},{10,12},{12... | collective-permute-start | bytes 786440 | tf_op jit(solution)/shard_map/ppermute | solution.py:109
  402.7 14.9 %collective-permute-start.14 = (bf16[256,512]{0,1:T(8,128)(2,1)}, bf16[256,512]{0,1:T(8,128)(2,1)}, u32[]{:S(2)}, u32[]{:S(2)}) collective-permute-start(bf16[256,512]{0,1:T(8,128)(2,1)} %collective-permute-done.13), channel_id=1, source_target_pairs={{0,2},{2,4},{4,6},{6,0},{1,3},{3,5},{5,7},{7,1},{8,10},{10,12},{12... | collective-permute-start | bytes 786440 | tf_op jit(solution)/shard_map/ppermute | solution.py:109
  414.0 9.5 %collective-permute-start.9 = (bf16[256,512]{0,1:T(8,128)(2,1)S(1)}, bf16[256,512]{0,1:T(8,128)(2,1)}, u32[]{:S(2)}, u32[]{:S(2)}) collective-permute-start(bf16[256,512]{0,1:T(8,128)(2,1)S(1)} %bitcast.107), channel_id=1, source_target_pairs={{0,6},{2,0},{4,2},{6,4},{1,7},{3,1},{5,3},{7,5},{8,14},{10,8},{12,... | collective-permute-start | bytes 786440 | tf_op jit(solution)/shard_map/ppermute | solution.py:112
  417.6 9.5 %collective-permute-start.8 = (bf16[256,512]{0,1:T(8,128)(2,1)}, bf16[256,512]{0,1:T(8,128)(2,1)}, u32[]{:S(2)}, u32[]{:S(2)}) collective-permute-start(bf16[256,512]{0,1:T(8,128)(2,1)} %collective-permute-done.7), channel_id=1, source_target_pairs={{0,2},{2,4},{4,6},{6,0},{1,3},{3,5},{5,7},{7,1},{8,10},{10,12},{12... | collective-permute-start | bytes 786440 | tf_op jit(solution)/shard_map/ppermute | solution.py:109
  432.7 5.8 %copy-start = (bf16[1024,512]{1,0:T(8,128)(2,1)S(1)}, bf16[1024,512]{1,0:T(8,128)(2,1)}, u32[]{:S(2)}) copy-start(bf16[1024,512]{1,0:T(8,128)(2,1)} %copy.30) | copy-start | bytes 3145732
  445.0 0.7 copy-start.3
Sparse Core Ops, SparseCore 0:
  8.9 12.4 all-gather.1
  65.3 121.0 reduce-scatter.5
  189.5 120.7 reduce-scatter.3
  445.1 90.5 reduce-scatter.7
